TPU v7x, 256 devices: a whole 4x4x8 slice. The times are simulated.
256 devices in a mesh: group: 8 (over y, core), expert: 32 (over z, x).
Axes of the slice: x: 4, y: 4, z: 8, core: 2. Of those that a mesh axis runs over, the one named last changes fastest.
Arguments:
- context: bfloat16 [32768, 1024], P(('group', 'expert')), may hold values from -6 to 6
- residual: bfloat16 [32768, 2048], P(('group', 'expert')), may hold values from -0.8984375 to 0.8984375
- attn_out_w: bfloat16 [1024, 2048], P('group'), may hold values from -0.02734375 to 0.02734375
- norm_gain: float32 [2048], replicated, may hold values from 0.25 to 1.75
- router_w: bfloat16 [2048, 32], replicated, may hold values from -0.047851562 to 0.047851562
- shared_in: bfloat16 [2048, 2816], P('group'), may hold values from -0.125 to 0.125
- shared_out: bfloat16 [1408, 2048], P(None, 'group'), may hold values from -0.0234375 to 0.0234375
- expert_in: bfloat16 [32, 2048, 1536], P('expert'), may hold values from -0.125 to 0.125
- expert_out_w: bfloat16 [32, 768, 2048], P('expert'), may hold values from -0.21875 to 0.21875
- routes: int32 [32768, 6], P(('group', 'expert')), may hold values from 0 to 31, all different within a row; in each aligned block of 128 rows (0 to 127, 128 to 255, ...) at most 32 rows name the same one
Outputs:
- layer_out: bfloat16 [32768, 2048], P(('group', 'expert'))
Inputs may be any that keep to these rules, and one draw needn't show every extreme that they name: `routes`: the 6 experts of a token differ. Among the rows of one device, no expert is named by more than 32 rows, a bound that some block reaches.
All inputs are finite; a program needn't handle non-finite values.
Results may differ from a plain program's by a relative error of at most 0.022.
Values may be sent and summed in bfloat16 or wider, within the bound.
No kernel may reach another device: no remote copies, remote signals or barrier semaphores. Data moves between devices by JAX's collectives and lax.ppermute only.
A program may use at most 128 MiB of HBM per device.

v0:
```python
import jax
import jax.numpy as jnp
from jax import lax
from jax.sharding import PartitionSpec as P


def swiglu_rows(rows, w_in, w_out):
    width = w_out.shape[0]
    mid = jnp.dot(rows, w_in, preferred_element_type=jnp.float32)
    act = (jax.nn.silu(mid[:, :width]) * mid[:, width:]).astype(jnp.bfloat16)
    return jnp.dot(act, w_out, preferred_element_type=jnp.float32)


def per_device(
    context,
    residual,
    attn_out_w,
    norm_gain,
    router_w,
    shared_in,
    shared_out,
    expert_in,
    expert_out_w,
    routes,
):
    tok_rows = residual.shape[0]
    width = residual.shape[1]
    picks = routes.shape[1]
    experts = lax.axis_size("expert")
    capacity = 4 * tok_rows * picks // (3 * experts)
    columns = context
    attn = jnp.dot(
        columns,
        lax.all_gather(attn_out_w, "group", axis=0, tiled=True),
        preferred_element_type=jnp.float32,
    )
    hidden_state = (residual.astype(jnp.float32) + attn).astype(jnp.bfloat16)
    hidden_f = hidden_state.astype(jnp.float32)
    scale = lax.rsqrt(jnp.mean(hidden_f * hidden_f, axis=-1, keepdims=True) + 1e-06)
    normed = (hidden_f * scale * norm_gain).astype(jnp.bfloat16)
    logits = jnp.dot(normed, router_w, preferred_element_type=jnp.float32)
    chosen = routes[:, :, None] == jnp.arange(experts, dtype=jnp.int32)[None, None, :]
    picked = jnp.sum(jnp.where(chosen, logits[:, None, :], 0.0), axis=-1)
    sig = jax.nn.sigmoid(picked)
    gates = sig / jnp.sum(sig, axis=1, keepdims=True)
    flat_e = routes.reshape(-1)
    onehot = (flat_e[:, None] == jnp.arange(experts, dtype=jnp.int32)[None, :]).astype(jnp.int32)
    rank = jnp.cumsum(onehot, axis=0) - onehot
    position = jnp.sum(rank * onehot, axis=1)
    slot_of = flat_e * capacity + position
    token_of = jnp.arange(tok_rows * picks, dtype=jnp.int32) // picks
    source = jnp.zeros((experts * capacity,), jnp.int32).at[slot_of].set(token_of)
    filled = jnp.zeros((experts * capacity,), jnp.int32).at[slot_of].set(1)
    outgoing = jnp.where(filled[:, None] > 0, normed[source], jnp.zeros((), jnp.bfloat16))
    outgoing = outgoing.reshape(experts, capacity, width)
    local_in = expert_in[0]
    local_out = expert_out_w[0]
    arrived = lax.all_to_all(outgoing, "expert", split_axis=0, concat_axis=0, tiled=True)
    flat_rows = arrived.reshape(-1, width)
    returned = lax.all_to_all(
        swiglu_rows(flat_rows, local_in, local_out).astype(jnp.bfloat16).reshape(arrived.shape),
        "expert",
        split_axis=0,
        concat_axis=0,
        tiled=True,
    )
    gathered = returned.reshape(experts * capacity, width)[slot_of]
    weighted = gates.reshape(-1, 1) * gathered.astype(jnp.float32)
    routed = jnp.sum(weighted.reshape(tok_rows, picks, width), axis=1)
    shared_hidden = shared_out.shape[0]
    columns = normed
    shared_mid = jnp.dot(
        columns,
        lax.all_gather(shared_in, "group", axis=0, tiled=True),
        preferred_element_type=jnp.float32,
    )
    shared_act = (
        jax.nn.silu(shared_mid[:, :shared_hidden]) * shared_mid[:, shared_hidden:]
    ).astype(jnp.bfloat16)
    shared_y = jnp.dot(
        shared_act,
        lax.all_gather(shared_out, "group", axis=1, tiled=True),
        preferred_element_type=jnp.float32,
    )
    return (hidden_f + shared_y + routed).astype(jnp.bfloat16)


def solution(mesh):
    placed = (
        P(("group", "expert"), None),
        P(("group", "expert"), None),
        P("group", None),
        P(),
        P(),
        P("group", None),
        P(None, "group"),
        P("expert", None, None),
        P("expert", None, None),
        P(("group", "expert"), None),
    )
    return jax.shard_map(
        per_device,
        mesh=mesh,
        in_specs=placed,
        out_specs=P(("group", "expert"), None),
        check_vma=False,
    )
```

profile of v0, /device:TPU:2, one launch (start us, length us, event | category | flops | bytes accessed | tf_op | source)
XLA Modules:
  0.0 323.8 jit_solution(1857204493511975896)
XLA Ops:
  6.5 0.0 copy-start
  6.5 0.0 all-gather.4.cloned.1.call-start
  6.5 0.7 all-gather.4.cloned.1.call-update
  7.3 0.0 copy-start.6
  7.3 0.0 all-gather.6.cloned.1.call-start
  7.3 0.7 all-gather.6.cloned.1.call-update
  8.0 0.8 copy.21
  8.8 0.1 eq.45
  9.0 0.1 eq.41
  9.1 1.7 reduce-window.6
  10.9 0.3 slice_reduce_fusion
  11.1 0.7 broadcast_multiply_fusion
  11.8 0.1 copy.20
  12.0 0.1 mul.71
  12.1 0.1 fusion.15
  12.2 3.4 %scatter_custom_fusion.1 = s32[1024]{0:T(1024)S(1)} fusion(s32[768]{0:T(1024)S(1)} %fusion.21, s32[768]{0:T(1024)S(1)} %add_select_fusion, s32[]{:T(128)} %constant.16.clone.1), kind=kCustom, calls=%fused_computation.51 | custom fusion | bytes 4100 | tf_op jit(solution)/shard_map/scatter | solution.py:52
  15.6 3.4 %scatter_custom_fusion = s32[1024]{0:T(1024)S(1)} fusion(s32[768]{0:T(1024)S(1)} %fusion.21, s32[768]{0:T(1024)S(1)} %broadcast.97, s32[]{:T(128)} %constant.16.clone.1), kind=kCustom, calls=%fused_computation.54 | custom fusion | bytes 4100 | tf_op jit(solution)/shard_map/scatter | solution.py:53
  19.0 0.1 broadcast_in_dim.46
  19.1 27.8 %all-gather.4.cloned.1.call-done = bf16[1024,2048]{1,0:T(8,128)(2,1)} async-done(((bf16[128,2048]{1,0:T(8,128)(2,1)}), bf16[1024,2048]{1,0:T(8,128)(2,1)}) %all-gather.4.cloned.1.call-update) | async-done | bytes 4194320 | tf_op jit(solution)/shard_map/all_gather | solution.py:34
  46.9 3.2 multiply_reduce_fusion.1
  50.1 0.0 copy-start.3
  50.1 0.9 copy-done.3
  51.1 0.0 copy-done.6
  51.1 1.0 multiply_convert_fusion
  52.0 9.9 %gather_fusion = bf16[1024,2048]{1,0:T(8,128)(2,1)} fusion(bf16[128,2048]{1,0:T(8,128)(2,1)} %multiply_convert_fusion, s32[1024]{0:T(1024)S(1)} %fusion.19), kind=kCustom, calls=%fused_computation | custom fusion | bytes 8392704 | tf_op jit(solution)/shard_map/gather | solution.py:54
  62.0 5.2 %broadcast_select_fusion = bf16[32,32,2048]{2,1,0:T(8,128)(2,1)} fusion(bf16[32,32,2048]{2,1,0:T(8,128)(2,1)} %bitcast.38, pred[32,32]{1,0:T(8,128)(4,1)S(1)} %broadcast_in_dim.46), kind=kLoop, calls=%fused_computation.7 | loop fusion | flops 2097152 | bytes 8389632 | tf_op jit(solution)/shard_map/jit(_where)/select_n | solution.py:54
  67.2 10.2 %all-to-all-start = ((bf16[32,32,2048]{2,1,0:T(8,128)(2,1)}), bf16[32,32,2048]{2,1,0:T(8,128)(2,1)}, u32[]{:S(2)}, u32[]{:S(2)}) async-start(bf16[32,32,2048]{2,1,0:T(8,128)(2,1)} %broadcast_select_fusion), calls=%async_computation | async-start | bytes 8388608 | tf_op jit(solution)/shard_map/all_to_all | solution.py:58
  77.4 0.0 all-gather.8.cloned.1.call-start
  77.4 0.7 all-gather.8.cloned.1.call-update
  78.1 97.0 %all-to-all-done = bf16[32,32,2048]{2,1,0:T(8,128)(2,1)} async-done(((bf16[32,32,2048]{2,1,0:T(8,128)(2,1)}), bf16[32,32,2048]{2,1,0:T(8,128)(2,1)}, u32[]{:S(2)}, u32[]{:S(2)}) %all-to-all-start) | async-done | bytes 4194336 | tf_op jit(solution)/shard_map/all_to_all | solution.py:58
  175.1 10.0 %fusion = f32[1024,1536]{1,0:T(8,128)S(1)} fusion(bf16[1024,2048]{1,0:T(8,128)(2,1)} %bitcast.2, bf16[1,2048,1536]{2,1,0:T(8,128)(2,1)} %param.17), kind=kOutput, calls=%fused_computation.5 | convolution fusion | flops 6442450944 | bytes 16777216 | tf_op jit(solution)/shard_map/dot_general | solution.py:9
  185.2 0.0 copy-done
  185.2 5.1 %convolution_convert_fusion = bf16[1024,2048]{1,0:T(8,128)(2,1)} fusion(bf16[1,768,2048]{2,1,0:T(8,128)(2,1)S(1)} %copy-done, f32[1024,1536]{1,0:T(8,128)S(1)} %fusion), kind=kOutput, calls=%fused_computation.8 | convolution fusion | flops 3228041216 | bytes 13631488 | tf_op jit(solution)/shard_map/dot_general | solution.py:11
  190.3 0.0 copy-start.2
  190.3 0.0 copy-start.4
  190.3 0.0 copy-start.5
  190.3 5.0 %all-to-all-start.1 = ((bf16[32,32,2048]{2,1,0:T(8,128)(2,1)}), bf16[32,32,2048]{2,1,0:T(8,128)(2,1)}, u32[]{:S(2)}, u32[]{:S(2)}) async-start(bf16[32,32,2048]{2,1,0:T(8,128)(2,1)} %bitcast.39), calls=%async_computation.1 | async-start | bytes 8388608 | tf_op jit(solution)/shard_map/all_to_all | solution.py:60
  195.2 0.0 copy-done.2
  195.3 0.0 copy-done.4
  195.3 0.3 fusion.29
  195.5 0.0 copy-done.5
  195.6 0.1 copy.19
  195.7 0.0 all-gather.6.cloned.1.call-done
  195.8 7.1 %fusion.28 = f32[128,2816]{1,0:T(8,128)} fusion(bf16[128,2048]{1,0:T(8,128)(2,1)S(1)} %copy-done.2, bf16[2048,2816]{1,0:T(8,128)(2,1)} %all-gather.6.cloned.1.call-done), kind=kOutput, calls=%fused_computation.59 | convolution fusion | flops 1476395008 | bytes 13500416 | tf_op jit(solution)/shard_map/dot_general | solution.py:72
  202.9 88.4 %all-to-all-done.1 = bf16[32,32,2048]{2,1,0:T(8,128)(2,1)} async-done(((bf16[32,32,2048]{2,1,0:T(8,128)(2,1)}), bf16[32,32,2048]{2,1,0:T(8,128)(2,1)}, u32[]{:S(2)}, u32[]{:S(2)}) %all-to-all-start.1) | async-done | bytes 4194336 | tf_op jit(solution)/shard_map/all_to_all | solution.py:60
  291.3 9.1 %gather_fusion.1 = bf16[768,2048]{1,0:T(8,128)(2,1)S(1)} fusion(bf16[1024,2048]{1,0:T(8,128)(2,1)} %bitcast.6, s32[1024]{0:T(1024)S(1)} %pad_clamp_fusion), kind=kCustom, calls=%fused_computation.1 | custom fusion | bytes 6294528 | tf_op jit(solution)/shard_map/gather | solution.py:67
  300.3 3.7 %reshape.103 = f32[128,6,2048]{2,1,0:T(8,128)} reshape(bf16[768,2048]{1,0:T(8,128)(2,1)S(1)} %gather_fusion.1) | data formatting | bytes 9437184 | tf_op jit(solution)/shard_map/convert_element_type | solution.py:68
  304.0 0.0 copy-start.1
  304.0 7.8 %multiply_reduce_fusion = f32[128,2048]{1,0:T(8,128)} fusion(f32[128,6,2048]{2,1,0:T(8,128)} %reshape.103, f32[128,6]{1,0:T(8,128)S(1)} %copy.19), kind=kLoop, calls=%fused_computation.4 | loop fusion | flops 2883584 | bytes 7343104 | tf_op jit(solution)/shard_map/reduce_sum | solution.py:69
  311.8 0.0 all-gather.8.cloned.1.call-done
  311.8 5.5 %fusion.5 = bf16[128,2048]{1,0:T(8,128)(2,1)} fusion(f32[128,2048]{1,0:T(8,128)} %multiply_reduce_fusion, f32[128,2048]{1,0:T(8,128)} %copy-done.3, bf16[1408,2048]{1,0:T(8,128)(2,1)} %all-gather.8.cloned.1.call-done, f32[128,2816]{1,0:T(8,128)} %fusion.28), kind=kOutput, calls=%fused_computation.15 | convolution fusion | flops 740065280 | bytes 9830400 | tf_op jit(solution)/shard_map/dot_general | solution.py:80
  317.3 0.0 copy-done.1
  (12 shorter events, 0.1 us)
Async XLA Ops:
  6.5 178.6 %copy-start = (bf16[1,768,2048]{2,1,0:T(8,128)(2,1)S(1)}, bf16[1,768,2048]{2,1,0:T(8,128)(2,1)}, u32[]{:S(2)}) copy-start(bf16[1,768,2048]{2,1,0:T(8,128)(2,1)} %param.18) | copy-start | bytes 9437188
  6.5 40.4 %all-gather.4.cloned.1.call-start = ((), (), s32[]{:S(2)}) async-start(), calls=%async_computation.2 | async-start | bytes 4718592 | tf_op jit(solution)/shard_map/all_gather | solution.py:34
  7.3 43.8 %copy-start.6 = (f32[2048]{0:T(1024)S(1)}, f32[2048]{0:T(1024)}, u32[]{:S(2)}) copy-start(f32[2048]{0:T(1024)} %param.13) | copy-start | bytes 24580
  7.3 188.5 %all-gather.6.cloned.1.call-start = ((), (), s32[]{:S(2)}) async-start(), calls=%async_computation.3 | async-start | bytes 12976128 | tf_op jit(solution)/shard_map/all_gather | solution.py:74
  50.1 1.0 copy-start.3
  67.2 108.0 %all-to-all-start = ((bf16[32,32,2048]{2,1,0:T(8,128)(2,1)}), bf16[32,32,2048]{2,1,0:T(8,128)(2,1)}, u32[]{:S(2)}, u32[]{:S(2)}) async-start(bf16[32,32,2048]{2,1,0:T(8,128)(2,1)} %broadcast_select_fusion), calls=%async_computation | async-start | bytes 8388608 | tf_op jit(solution)/shard_map/all_to_all | solution.py:58
  77.4 234.4 %all-gather.8.cloned.1.call-start = ((), (), s32[]{:S(2)}) async-start(), calls=%async_computation.4 | async-start | bytes 6488064 | tf_op jit(solution)/shard_map/all_gather | solution.py:82
  190.3 5.0 %copy-start.2 = (bf16[128,2048]{1,0:T(8,128)(2,1)S(1)}, bf16[128,2048]{1,0:T(8,128)(2,1)}, u32[]{:S(2)}) copy-start(bf16[128,2048]{1,0:T(8,128)(2,1)} %multiply_convert_fusion) | copy-start | bytes 1572868
  190.3 5.0 %copy-start.4 = (bf16[2048,32]{0,1:T(8,128)(2,1)S(1)}, bf16[2048,32]{0,1:T(8,128)(2,1)}, u32[]{:S(2)}) copy-start(bf16[2048,32]{0,1:T(8,128)(2,1)} %param.14) | copy-start | bytes 393220
  190.3 5.3 %copy-start.5 = (s32[128,6]{0,1:T(8,128)S(1)}, s32[128,6]{0,1:T(8,128)}, u32[]{:S(2)}) copy-start(s32[128,6]{0,1:T(8,128)} %param.19) | copy-start | bytes 9220
  190.3 101.0 %all-to-all-start.1 = ((bf16[32,32,2048]{2,1,0:T(8,128)(2,1)}), bf16[32,32,2048]{2,1,0:T(8,128)(2,1)}, u32[]{:S(2)}, u32[]{:S(2)}) async-start(bf16[32,32,2048]{2,1,0:T(8,128)(2,1)} %bitcast.39), calls=%async_computation.1 | async-start | bytes 8388608 | tf_op jit(solution)/shard_map/all_to_all | solution.py:60
  304.0 13.3 %copy-start.1 = (bf16[1,768,2048]{2,1,0:T(8,128)(2,1)S(1)}, bf16[1,768,2048]{2,1,0:T(8,128)(2,1)}, u32[]{:S(2)}) copy-start(bf16[1,768,2048]{2,1,0:T(8,128)(2,1)} %param.18) | copy-start | bytes 9437188
Sparse Core Ops, SparseCore 0:
  9.2 37.6 all-gather.3
  48.7 65.4 all-gather.5
  116.1 45.6 all-gather.7
where the time goes:
time: 324 us
  waiting for transfers between devices  215 us (66%)
  local copies, waits for them, and re-layouts  32.2 us (10%)
  matrix products  31.2 us (10%)
  other arithmetic  16.6 us (5%)
  starting transfers between devices  15.2 us (5%)
  between operations  13.3 us (4%)
    all_to_all x1, waiting for transfers between devices, per_device(): lax.all_to_all(outgoing, 'expert', split_axis=0, concat_axis=0, tiled=True)  97 us
    all_to_all x1, waiting for transfers between devices, per_device(): lax.all_to_all(swiglu_rows(flat_rows, local_in, local_out).astype(jnp.bfl...  88.4 us
    all_gather x1, waiting for transfers between devices, per_device(): lax.all_gather(attn_out_w, 'group', axis=0, tiled=True)  27.8 us
    all_to_all x1, starting transfers between devices, per_device(): lax.all_to_all(outgoing, 'expert', split_axis=0, concat_axis=0, tiled=True)  10.2 us
    dot_general x1, matrix products, swiglu_rows(): mid = jnp.dot(rows, w_in, preferred_element_type=jnp.float32)  10 us
    gather x1, local copies, waits for them, and re-layouts, per_device(): normed[source]  9.94 us
    gather x1, local copies, waits for them, and re-layouts, per_device(): gathered = returned.reshape(experts * capacity, width)[slot_of]  9.06 us
    reduce_sum x1, other arithmetic, per_device(): routed = jnp.sum(weighted.reshape(tok_rows, picks, width), axis=1)  7.77 us
  transfers between devices with their start and end apart: 5, of which 3 were waited for; matrix products, arithmetic and copies ran while one was open for 23% of the time, Pallas kernels for 0%

commit v1 on v0

--- a/solution.py
+++ b/solution.py
@@ -31,7 +31,15 @@
     columns = context
     attn = jnp.dot(
         columns,
-        lax.all_gather(attn_out_w, "group", axis=0, tiled=True),
+        jnp.concatenate(
+            jax.lax.all_to_all(
+                jnp.stack([attn_out_w for _ in range(jax.lax.axis_size("group"))], 0),
+                axis_name="group",
+                split_axis=0,
+                concat_axis=0,
+            ),
+            axis=0,
+        ),
         preferred_element_type=jnp.float32,
     )
     hidden_state = (residual.astype(jnp.float32) + attn).astype(jnp.bfloat16)

time: 324 us -> 384 us (1.19)
  waiting for transfers between devices: 215 us -> 261 us
  starting transfers between devices: 15.2 us -> 26 us
    all_to_all x0 -> x1, waiting for transfers between devices: none -> 75.9 us  [per_device(): jax.lax.all_to_all(jnp.stack([attn_out_w for _ in range(jax.lax.axis_size...]
    all_gather x1 -> x0, waiting for transfers between devices: 27.8 us -> none  [per_device(): lax.all_gather(attn_out_w, 'group', axis=0, tiled=True)]
    all_to_all x1, waiting for transfers between devices: 97 us -> 91.5 us  [per_device(): lax.all_to_all(outgoing, 'expert', split_axis=0, concat_axis=0, tiled=True)]
    all_to_all x0 -> x1, starting transfers between devices: none -> 4.68 us  [per_device(): jax.lax.all_to_all(jnp.stack([attn_out_w for _ in range(jax.lax.axis_size...]
  transfers between devices with their start and end apart: 5 -> 5, of which waited for: 3 -> 3; matrix products, arithmetic and copies ran while one was open for 23% -> 20% of each run, Pallas kernels for 0% -> 0%
where the time goes in v1:
time: 384 us; the launch traced here: 382 us
  waiting for transfers between devices  261 us (68%)
  local copies, waits for them, and re-layouts  35.5 us (9%)
  matrix products  31.4 us (8%)
  starting transfers between devices  26 us (7%)
  other arithmetic  15.1 us (4%)
  between operations  13.6 us (4%)
    all_to_all x1, waiting for transfers between devices, per_device(): lax.all_to_all(swiglu_rows(flat_rows, local_in, local_out).astype(jnp.bfl...  91.8 us
    all_to_all x1, waiting for transfers between devices, per_device(): lax.all_to_all(outgoing, 'expert', split_axis=0, concat_axis=0, tiled=True)  91.5 us
    all_to_all x1, waiting for transfers between devices, per_device(): jax.lax.all_to_all(jnp.stack([attn_out_w for _ in range(jax.lax.axis_size...  75.9 us
    all_to_all x1, starting transfers between devices, per_device(): lax.all_to_all(outgoing, 'expert', split_axis=0, concat_axis=0, tiled=True)  13.3 us
    dot_general x1, matrix products, swiglu_rows(): mid = jnp.dot(rows, w_in, preferred_element_type=jnp.float32)  10 us
    gather x1, local copies, waits for them, and re-layouts, per_device(): normed[source]  9.95 us
    gather x1, local copies, waits for them, and re-layouts, per_device(): gathered = returned.reshape(experts * capacity, width)[slot_of]  9.06 us
    all_to_all x1, starting transfers between devices, per_device(): lax.all_to_all(swiglu_rows(flat_rows, local_in, local_out).astype(jnp.bfl...  8.02 us
  transfers between devices with their start and end apart: 5, of which 3 were waited for; matrix products, arithmetic and copies ran while one was open for 20% of the time, Pallas kernels for 0%

profile of v1, /device:TPU:2, one launch (start us, length us, event | category | flops | bytes accessed | tf_op | source)
XLA Modules:
  0.0 382.3 jit_solution(2747298494307702113)
XLA Ops:
  6.5 0.0 copy-start
  6.5 0.0 all-gather.3.cloned.1.call-start
  6.5 0.7 all-gather.3.cloned.1.call-update
  7.3 3.8 stack.2
  11.0 0.0 copy-start.5
  11.0 4.7 %all-to-all-start = ((bf16[8,128,2048]{2,1,0:T(8,128)(2,1)}), bf16[8,128,2048]{2,1,0:T(8,128)(2,1)}, u32[]{:S(2)}, u32[]{:S(2)}) async-start(bf16[8,128,2048]{2,1,0:T(8,128)(2,1)} %stack.2), calls=%async_computation | async-start | bytes 8388608 | tf_op jit(solution)/shard_map/all_to_all | solution.py:35
  15.7 0.0 copy-done.5
  15.7 0.0 copy-start.6
  15.7 0.1 copy.21
  15.9 0.1 eq.45
  16.0 0.1 eq.41
  16.1 1.7 reduce-window.6
  17.9 0.3 slice_reduce_fusion
  18.2 0.1 copy.20
  18.3 0.1 mul.71
  18.5 0.1 fusion.15
  18.6 3.4 scatter_custom_fusion.1
  22.0 3.4 scatter_custom_fusion
  25.4 0.1 broadcast_in_dim.46
  25.5 75.9 %all-to-all-done = bf16[8,128,2048]{2,1,0:T(8,128)(2,1)} async-done(((bf16[8,128,2048]{2,1,0:T(8,128)(2,1)}), bf16[8,128,2048]{2,1,0:T(8,128)(2,1)}, u32[]{:S(2)}, u32[]{:S(2)}) %all-to-all-start) | async-done | bytes 4194336 | tf_op jit(solution)/shard_map/all_to_all | solution.py:35
  101.4 3.2 multiply_reduce_fusion.1
  104.6 0.0 copy-start.3
  104.7 1.0 copy-done.3
  105.7 0.0 copy-done.6
  105.7 1.0 multiply_convert_fusion
  106.6 9.9 %gather_fusion = bf16[1024,2048]{1,0:T(8,128)(2,1)} fusion(bf16[128,2048]{1,0:T(8,128)(2,1)} %multiply_convert_fusion, s32[1024]{0:T(1024)S(1)} %fusion.19), kind=kCustom, calls=%fused_computation | custom fusion | bytes 8392704 | tf_op jit(solution)/shard_map/gather | solution.py:62
  116.6 4.6 %broadcast_select_fusion = bf16[32,32,2048]{2,1,0:T(8,128)(2,1)} fusion(bf16[32,32,2048]{2,1,0:T(8,128)(2,1)} %bitcast.39, pred[32,32]{1,0:T(8,128)(4,1)S(1)} %broadcast_in_dim.46), kind=kLoop, calls=%fused_computation.7 | loop fusion | flops 2097152 | bytes 8389632 | tf_op jit(solution)/shard_map/jit(_where)/select_n | solution.py:62
  121.2 13.3 %all-to-all-start.1 = ((bf16[32,32,2048]{2,1,0:T(8,128)(2,1)}), bf16[32,32,2048]{2,1,0:T(8,128)(2,1)}, u32[]{:S(2)}, u32[]{:S(2)}) async-start(bf16[32,32,2048]{2,1,0:T(8,128)(2,1)} %broadcast_select_fusion), calls=%async_computation.1 | async-start | bytes 8388608 | tf_op jit(solution)/shard_map/all_to_all | solution.py:66
  134.4 0.0 all-gather.5.cloned.1.call-start
  134.5 0.7 all-gather.5.cloned.1.call-update
  135.2 91.5 %all-to-all-done.1 = bf16[32,32,2048]{2,1,0:T(8,128)(2,1)} async-done(((bf16[32,32,2048]{2,1,0:T(8,128)(2,1)}), bf16[32,32,2048]{2,1,0:T(8,128)(2,1)}, u32[]{:S(2)}, u32[]{:S(2)}) %all-to-all-start.1) | async-done | bytes 4194336 | tf_op jit(solution)/shard_map/all_to_all | solution.py:66
  226.7 10.0 %fusion = f32[1024,1536]{1,0:T(8,128)S(1)} fusion(bf16[1024,2048]{1,0:T(8,128)(2,1)} %bitcast.3, bf16[1,2048,1536]{2,1,0:T(8,128)(2,1)} %param.17), kind=kOutput, calls=%fused_computation.5 | convolution fusion | flops 6442450944 | bytes 16777216 | tf_op jit(solution)/shard_map/dot_general | solution.py:9
  236.7 0.0 copy-done
  236.7 5.1 %convolution_convert_fusion = bf16[1024,2048]{1,0:T(8,128)(2,1)} fusion(bf16[1,768,2048]{2,1,0:T(8,128)(2,1)S(1)} %copy-done, f32[1024,1536]{1,0:T(8,128)S(1)} %fusion), kind=kOutput, calls=%fused_computation.8 | convolution fusion | flops 3228041216 | bytes 13631488 | tf_op jit(solution)/shard_map/dot_general | solution.py:11
  241.8 0.0 copy-start.2
  241.8 0.0 copy-start.4
  241.8 8.0 %all-to-all-start.2 = ((bf16[32,32,2048]{2,1,0:T(8,128)(2,1)}), bf16[32,32,2048]{2,1,0:T(8,128)(2,1)}, u32[]{:S(2)}, u32[]{:S(2)}) async-start(bf16[32,32,2048]{2,1,0:T(8,128)(2,1)} %bitcast.40), calls=%async_computation.2 | async-start | bytes 8388608 | tf_op jit(solution)/shard_map/all_to_all | solution.py:68
  249.8 0.0 copy-done.2
  249.8 0.0 copy-done.4
  249.8 0.3 fusion.29
  250.2 0.1 copy.19
  250.3 91.8 %all-to-all-done.2 = bf16[32,32,2048]{2,1,0:T(8,128)(2,1)} async-done(((bf16[32,32,2048]{2,1,0:T(8,128)(2,1)}), bf16[32,32,2048]{2,1,0:T(8,128)(2,1)}, u32[]{:S(2)}, u32[]{:S(2)}) %all-to-all-start.2) | async-done | bytes 4194336 | tf_op jit(solution)/shard_map/all_to_all | solution.py:68
  342.2 9.1 %gather_fusion.1 = bf16[768,2048]{1,0:T(8,128)(2,1)S(1)} fusion(bf16[1024,2048]{1,0:T(8,128)(2,1)} %bitcast.7, s32[1024]{0:T(1024)S(1)} %pad_clamp_fusion), kind=kCustom, calls=%fused_computation.1 | custom fusion | bytes 6294528 | tf_op jit(solution)/shard_map/gather | solution.py:75
  351.2 3.8 reshape.109
  355.0 7.6 %multiply_reduce_fusion = f32[128,2048]{1,0:T(8,128)} fusion(f32[128,6,2048]{2,1,0:T(8,128)} %reshape.109, f32[128,6]{1,0:T(8,128)S(1)} %copy.19), kind=kLoop, calls=%fused_computation.4 | loop fusion | flops 2883584 | bytes 7343104 | tf_op jit(solution)/shard_map/reduce_sum | solution.py:77
  362.6 0.0 all-gather.3.cloned.1.call-done
  362.6 0.0 copy-start.1
  362.6 7.4 %fusion.28 = f32[128,2816]{1,0:T(8,128)} fusion(bf16[128,2048]{1,0:T(8,128)(2,1)} %multiply_convert_fusion, bf16[2048,2816]{1,0:T(8,128)(2,1)} %all-gather.3.cloned.1.call-done), kind=kOutput, calls=%fused_computation.59 | convolution fusion | flops 1476395008 | bytes 13500416 | tf_op jit(solution)/shard_map/dot_general | solution.py:80
  370.0 0.0 all-gather.5.cloned.1.call-done
  370.0 5.5 %fusion.5 = bf16[128,2048]{1,0:T(8,128)(2,1)} fusion(f32[128,2048]{1,0:T(8,128)} %multiply_reduce_fusion, f32[128,2048]{1,0:T(8,128)} %copy-done.3, bf16[1408,2048]{1,0:T(8,128)(2,1)} %all-gather.5.cloned.1.call-done, f32[128,2816]{1,0:T(8,128)} %fusion.28), kind=kOutput, calls=%fused_computation.15 | convolution fusion | flops 740065280 | bytes 9830400 | tf_op jit(solution)/shard_map/dot_general | solution.py:88
  375.5 0.0 copy-done.1
  (13 shorter events, 0.2 us)
Async XLA Ops:
  6.5 230.2 %copy-start = (bf16[1,768,2048]{2,1,0:T(8,128)(2,1)S(1)}, bf16[1,768,2048]{2,1,0:T(8,128)(2,1)}, u32[]{:S(2)}) copy-start(bf16[1,768,2048]{2,1,0:T(8,128)(2,1)} %param.18) | copy-start | bytes 9437188
  6.5 356.0 %all-gather.3.cloned.1.call-start = ((), (), s32[]{:S(2)}) async-start(), calls=%async_computation.3 | async-start | bytes 12976128 | tf_op jit(solution)/shard_map/all_gather | solution.py:82
  11.0 4.7 %copy-start.5 = (s32[128,6]{0,1:T(8,128)S(1)}, s32[128,6]{0,1:T(8,128)}, u32[]{:S(2)}) copy-start(s32[128,6]{0,1:T(8,128)} %param.19) | copy-start | bytes 9220
  11.0 90.4 %all-to-all-start = ((bf16[8,128,2048]{2,1,0:T(8,128)(2,1)}), bf16[8,128,2048]{2,1,0:T(8,128)(2,1)}, u32[]{:S(2)}, u32[]{:S(2)}) async-start(bf16[8,128,2048]{2,1,0:T(8,128)(2,1)} %stack.2), calls=%async_computation | async-start | bytes 8388608 | tf_op jit(solution)/shard_map/all_to_all | solution.py:35
  15.7 90.0 %copy-start.6 = (f32[2048]{0:T(1024)S(1)}, f32[2048]{0:T(1024)}, u32[]{:S(2)}) copy-start(f32[2048]{0:T(1024)} %param.13) | copy-start | bytes 24580
  104.6 1.0 copy-start.3
  121.2 105.5 %all-to-all-start.1 = ((bf16[32,32,2048]{2,1,0:T(8,128)(2,1)}), bf16[32,32,2048]{2,1,0:T(8,128)(2,1)}, u32[]{:S(2)}, u32[]{:S(2)}) async-start(bf16[32,32,2048]{2,1,0:T(8,128)(2,1)} %broadcast_select_fusion), calls=%async_computation.1 | async-start | bytes 8388608 | tf_op jit(solution)/shard_map/all_to_all | solution.py:66
  134.4 235.5 %all-gather.5.cloned.1.call-start = ((), (), s32[]{:S(2)}) async-start(), calls=%async_computation.4 | async-start | bytes 6488064 | tf_op jit(solution)/shard_map/all_gather | solution.py:90
  241.8 8.1 %copy-start.2 = (bf16[128,2048]{1,0:T(8,128)(2,1)S(1)}, bf16[128,2048]{1,0:T(8,128)(2,1)}, u32[]{:S(2)}) copy-start(bf16[128,2048]{1,0:T(8,128)(2,1)} %multiply_convert_fusion) | copy-start | bytes 1572868
  241.8 8.1 %copy-start.4 = (bf16[2048,32]{0,1:T(8,128)(2,1)S(1)}, bf16[2048,32]{0,1:T(8,128)(2,1)}, u32[]{:S(2)}) copy-start(bf16[2048,32]{0,1:T(8,128)(2,1)} %param.14) | copy-start | bytes 393220
  241.8 100.4 %all-to-all-start.2 = ((bf16[32,32,2048]{2,1,0:T(8,128)(2,1)}), bf16[32,32,2048]{2,1,0:T(8,128)(2,1)}, u32[]{:S(2)}, u32[]{:S(2)}) async-start(bf16[32,32,2048]{2,1,0:T(8,128)(2,1)} %bitcast.40), calls=%async_computation.2 | async-start | bytes 8388608 | tf_op jit(solution)/shard_map/all_to_all | solution.py:68
  362.6 12.9 %copy-start.1 = (bf16[1,768,2048]{2,1,0:T(8,128)(2,1)S(1)}, bf16[1,768,2048]{2,1,0:T(8,128)(2,1)}, u32[]{:S(2)}) copy-start(bf16[1,768,2048]{2,1,0:T(8,128)(2,1)} %param.18) | copy-start | bytes 9437188
Sparse Core Ops, SparseCore 0:
  9.2 104.0 all-gather.2
  137.1 43.7 all-gather.4
